TPU v7x, 32 devices: a whole 2x2x4 slice. The times are simulated.
32 devices in a mesh: led: 4 (over y, x), row: 8 (over z, core).
Axes of the slice: x: 2, y: 2, z: 4, core: 2. Of those that a mesh axis runs over, the one named last changes fastest.
Arguments:
- spectrum: float32 [2, 4096, 4096], P(None, 'led', 'row'), may hold values from -6 to 6
- amplitudes: float32 [4, 2048, 2048], P('led', 'row'), may hold values from 0.2 to 3
- offsets: int32 [4, 2], replicated, may hold values from 0 to 2048
- coeffs: float32 [6], replicated, may hold values from -2.5 to 2.5
Outputs:
- updated: float32 [2, 4096, 4096], P(None, 'led', 'row')
All inputs are finite; a program needn't handle non-finite values.
Results may differ from a plain program's by a relative error of at most 0.0001.
Values sent between devices are 32-bit elements; how exact they have to be, the bound alone decides.
No kernel may reach another device: no remote copies, remote signals or barrier semaphores. Data moves between devices by JAX's collectives and lax.ppermute only.
A program may use at most 128 MiB of HBM per device.

v0:
```python
import math
import jax
import jax.numpy as jnp
from jax import lax
from jax.sharding import PartitionSpec as P

SOFTENING = 0.1
HIGHEST_PRECISION = lax.Precision.HIGHEST


def pupil_at(down_index, across_index, coeffs, centre):
    offset_down = down_index - centre
    offset_across = across_index - centre
    inside = offset_down * offset_down + offset_across * offset_across < centre * centre
    upper_norm = offset_down.astype(jnp.float32) * (1.0 / centre)
    lateral = offset_across.astype(jnp.float32) * (1.0 / centre)
    radial = upper_norm * upper_norm + lateral * lateral
    phases = (
        coeffs[0] * (2.0 * radial - 1.0)
        + coeffs[1] * (upper_norm * upper_norm - lateral * lateral)
        + coeffs[2] * (2.0 * upper_norm * lateral)
        + (3.0 * radial - 2.0) * (coeffs[3] * upper_norm + coeffs[4] * lateral)
        + coeffs[5] * (6.0 * radial * radial - 6.0 * radial + 1.0)
    )
    weight = jnp.where(inside, 1.0, 0.0).astype(jnp.float32)
    return (weight * jnp.cos(phases), weight * jnp.sin(phases))


def tables(outer_size, inner_size, direction):
    length = outer_size * inner_size
    angle_step = direction * 2.0 * math.pi / length
    first_index = jnp.arange(outer_size, dtype=jnp.int32)
    grid_first = first_index[:, None] * first_index[None, :] * inner_size % length
    angles_first = grid_first.astype(jnp.float32) * angle_step
    index_k = jnp.arange(outer_size, dtype=jnp.int32)[:, None, None]
    index_r = jnp.arange(inner_size, dtype=jnp.int32)[None, :, None]
    index_j = jnp.arange(inner_size, dtype=jnp.int32)[None, None, :]
    grid_second = index_r * (index_k + outer_size * index_j) % length
    angles_second = grid_second.astype(jnp.float32) * angle_step
    return (
        jnp.cos(angles_first),
        jnp.sin(angles_first),
        jnp.cos(angles_second),
        jnp.sin(angles_second),
    )


def transform(paired, inputs, middle, output, outer_size, inner_size, direction):
    first_re, first_im, second_re, second_im = tables(outer_size, inner_size, direction)
    scaling = 1.0 / math.sqrt(outer_size * inner_size)
    first_table = jnp.stack([jnp.stack([first_re, first_im]), jnp.stack([-first_im, first_re])])
    second_table = (
        jnp.stack([jnp.stack([second_re, second_im]), jnp.stack([-second_im, second_re])]) * scaling
    )
    middle_pair = jnp.einsum(
        "p" + inputs + ",pqtk->q" + middle, paired, first_table, precision=HIGHEST_PRECISION
    )
    return jnp.einsum(
        "p" + middle + ",pqkrj->q" + output, middle_pair, second_table, precision=HIGHEST_PRECISION
    )


def correct(field_re, field_im, measured):
    magnitude = jnp.sqrt(field_re * field_re + field_im * field_im + SOFTENING)
    factor = measured / magnitude
    return (field_re * factor - field_re, field_im * factor - field_im)


def on_device(spectrum, amplitudes, offsets, coeffs):
    led_count = lax.axis_size("led")
    row_count = lax.axis_size("row")
    led_index = lax.axis_index("led")
    row_index = lax.axis_index("row")
    size_rows = spectrum.shape[1]
    size_cols = spectrum.shape[2]
    window = amplitudes.shape[2]
    centre = window // 2
    block_rows = window // row_count
    outer_rows = window // led_count
    outer_cols = window // row_count
    row_shift = offsets[led_index, 0]
    col_shift = offsets[led_index, 1]
    measured = amplitudes[0]
    shape_cols = (2, block_rows, outer_cols, row_count)
    region = lax.all_gather(spectrum, "led", axis=1, tiled=True)
    band_rows = lax.dynamic_slice_in_dim(region, row_shift, window, 1)
    row_ids = jnp.arange(window, dtype=jnp.int32)[:, None]
    col_ids = (row_index * size_cols + jnp.arange(size_cols, dtype=jnp.int32))[None, :] - col_shift
    pupil_re, pupil_im = pupil_at(row_ids, col_ids, coeffs, centre)
    lit_re = pupil_re * band_rows[0] - pupil_im * band_rows[1]
    lit_im = pupil_re * band_rows[1] + pupil_im * band_rows[0]
    shape_rows = (2, outer_rows, led_count, size_cols)
    half = transform(
        jnp.stack([lit_re, lit_im]).reshape(shape_rows),
        "trc",
        "krc",
        "jkc",
        outer_rows,
        led_count,
        1.0,
    )
    stacked = half.reshape(2, window, size_cols)
    spread = lax.all_to_all(stacked, "row", split_axis=1, concat_axis=2, tiled=True)
    window_part = lax.dynamic_slice_in_dim(spread, col_shift, window, 2)
    field = transform(
        window_part.reshape(shape_cols), "ytr", "ykr", "yjk", outer_cols, row_count, 1.0
    )
    field = field.reshape(2, block_rows, window)
    diff_re, diff_im = correct(field[0], field[1], measured)
    back = transform(
        jnp.stack([diff_re, diff_im]).reshape(shape_cols),
        "ytr",
        "ykr",
        "yjk",
        outer_cols,
        row_count,
        -1.0,
    )
    padded = jnp.zeros((2, block_rows, row_count * size_cols), jnp.float32)
    padded = lax.dynamic_update_slice_in_dim(
        padded, back.reshape(2, block_rows, window), col_shift, 2
    )
    gathered_cols = lax.all_to_all(padded, "row", split_axis=2, concat_axis=1, tiled=True)
    spec = transform(
        gathered_cols.reshape(shape_rows), "trc", "krc", "jkc", outer_rows, led_count, -1.0
    ).reshape(2, window, size_cols)
    upd_re = pupil_re * spec[0] + pupil_im * spec[1]
    upd_im = pupil_re * spec[1] - pupil_im * spec[0]
    embedded = jnp.zeros((2, size_rows * led_count, size_cols), jnp.float32)
    embedded = lax.dynamic_update_slice_in_dim(embedded, jnp.stack([upd_re, upd_im]), row_shift, 1)
    summed = lax.psum_scatter(embedded, "led", scatter_dimension=1, tiled=True)
    return spectrum + summed


def solution(mesh):
    return jax.shard_map(
        on_device,
        mesh=mesh,
        in_specs=(P(None, "led", "row"), P("led", "row", None), P(), P()),
        out_specs=P(None, "led", "row"),
        check_vma=False,
    )
```

profile of v0, /device:TPU:0, one launch (start us, length us, event | category | flops | bytes accessed | tf_op | source)
XLA Modules:
  0.0 1087.1 jit_solution(2746678404710610124)
XLA Ops:
  27.8 141.4 %all-gather.2.cloned.1.call-done = f32[2,4096,512]{2,1,0:T(8,128)} async-done(((f32[2,1024,512]{2,1,0:T(8,128)}), f32[2,4096,512]{2,1,0:T(8,128)}) %all-gather.2.cloned.1.call-update) | async-done | bytes 16777232 | tf_op jit(solution)/shard_map/all_gather | solution.py:85
  169.3 26.9 %multiply_subtract_fusion = (f32[1,2048,512]{2,1,0:T(8,128)}, f32[1,2048,512]{2,1,0:T(8,128)}) fusion(f32[2,4096,512]{2,1,0:T(8,128)} %all-gather.2.cloned.1.call-done, s32[]{:T(128)S(6)} %select_n.238, s32[]{:T(128)S(6)} %add.718, f32[]{:T(128)} %bitcast.6, f32[512]{0:T(512)S(1)} %get-tuple-element.53, f32[2048]{0:T(1024)S(1)} %get-tuple-element.58, ...), kind=kLoop, calls=%fused_computation.55 | loop fusion | flops 33554432 | bytes 16818200 | tf_op jit(solution)/shard_map/sub | solution.py:90
  196.1 7.9 stack.215
  204.1 5.5 copy.143
  209.6 7.7 stack.216
  221.4 28.3 %fusion.46 = f32[2,512,4,512,1]{3,1,2,0,4:T(8,128)} fusion(f32[1,512,4,512]{3,1,0,2:T(8,128)S(1)} %copy.144, f32[1,512,4,512]{3,1,0,2:T(8,128)S(1)} %copy-done.3, f32[1,2,512,512]{2,3,0,1:T(8,128)S(1)} %copy-done.4, f32[1,2,512,512]{2,3,0,1:T(8,128)S(1)} %get-tuple-element.17), kind=kOutput, calls=%fused_computation.58 | convolution fusion | flops 25772949504 | bytes 20971520 | tf_op jit(solution)/shard_map/ptrc,pqtk->qkrc/dot_general | solution.py:55
  249.7 32.7 %fusion.11 = f32[2,4,512,512]{3,1,0,2:T(4,128)S(1)} fusion(f32[2,2,512,4,4]{3,4,0,1,2:T(4,128)} %copy.145, f32[2,512,4,512,1]{3,1,2,0,4:T(8,128)} %fusion.46), kind=kOutput, calls=%fused_computation.19 | convolution fusion | flops 201326592 | bytes 16908288 | tf_op jit(solution)/shard_map/pkrc,pqkrj->qjkc/dot_general | solution.py:58
  282.4 4.9 copy.147
  287.2 16.5 %copy.148 = f32[2,2048,512]{2,0,1:T(2,128)} copy(f32[2,2048,512]{2,1,0:T(8,128)S(1)} %bitcast.186) | data formatting | bytes 16777216 | tf_op jit(solution)/shard_map/reshape | solution.py:102
  303.7 5.1 all-to-all-start
  327.6 165.1 %all-to-all-done = f32[2,2048,512]{2,0,1:T(2,128)} async-done(((f32[2,2048,512]{2,0,1:T(2,128)}), f32[2,2048,512]{2,0,1:T(2,128)}, u32[]{:S(2)}, u32[]{:S(2)}) %all-to-all-start) | async-done | bytes 8388640 | tf_op jit(solution)/shard_map/all_to_all | solution.py:103
  492.7 8.2 copy.149
  501.0 8.8 copy.150
  509.7 4.5 dynamic-slice_bitcast_fusion
  514.3 5.3 copy.151
  519.5 9.7 fusion.54
  529.3 7.0 fusion.47
  545.6 9.1 fusion.53
  554.8 7.0 fusion.50
  564.2 5.4 broadcast_in_dim.15
  569.6 12.4 %copy_dynamic-update-slice_fusion = f32[2,256,4096]{1,0,2:T(2,128)} fusion(f32[2,256,4096]{1,0,2:T(2,128)} %broadcast_in_dim.15, s32[]{:T(128)S(6)} %select_n.239, f32[2,256,2048]{1,2,0:T(8,128)S(1)} %bitcast.190), kind=kLoop, calls=%fused_computation.52 | loop fusion | bytes 8388612 | tf_op jit(solution)/shard_map/dynamic_update_slice | solution.py:120
  582.1 5.0 all-to-all-start.1
  600.4 170.5 %all-to-all-done.1 = f32[2,256,4096]{1,0,2:T(2,128)} async-done(((f32[2,256,4096]{1,0,2:T(2,128)}), f32[2,256,4096]{1,0,2:T(2,128)}, u32[]{:S(2)}, u32[]{:S(2)}) %all-to-all-start.1) | async-done | bytes 8388640 | tf_op jit(solution)/shard_map/all_to_all | solution.py:123
  770.9 7.3 copy.164
  778.2 13.3 %copy.165 = f32[2,8,256,512]{3,0,2,1:T(2,128)} copy(f32[2,8,256,512]{2,3,1,0:T(8,128)} %bitcast.188) | data formatting | bytes 16777216 | tf_op jit(solution)/shard_map/all_to_all | solution.py:123
  791.5 31.6 %fusion.41 = f32[2,512,4,512,1]{3,1,2,0,4:T(8,128)} fusion(f32[2,512,4,512]{3,0,2,1:T(2,128)} %bitcast.191, f32[1,2,512,512]{2,3,1,0:T(8,128)} %get-tuple-element.16, f32[1,2,512,512]{2,3,1,0:T(8,128)S(1)} %get-tuple-element.15), kind=kOutput, calls=%fused_computation.57 | convolution fusion | flops 25770852352 | bytes 20971520 | tf_op jit(solution)/shard_map/ptrc,pqtk->qkrc/dot_general | solution.py:55
  823.2 32.4 %fusion.14 = f32[2,4,512,512]{3,1,0,2:T(4,128)S(1)} fusion(f32[2,2,512,4,4]{3,4,0,1,2:T(4,128)} %copy.168, f32[2,512,4,512,1]{3,1,2,0,4:T(8,128)} %fusion.41), kind=kOutput, calls=%fused_computation.20 | convolution fusion | flops 201326592 | bytes 16908288 | tf_op jit(solution)/shard_map/pkrc,pqkrj->qjkc/dot_general | solution.py:58
  863.9 23.1 %fusion.32 = (f32[1,2048,512]{2,1,0:T(8,128)S(1)}, f32[1,2048,512]{2,1,0:T(8,128)S(1)}) fusion(f32[1,4,512,512]{3,2,1,0:T(8,128)S(1)} %copy.171, f32[1,4,512,512]{3,2,1,0:T(8,128)S(1)} %copy.170, f32[]{:T(128)} %bitcast.6, f32[512]{0:T(512)S(1)} %get-tuple-element.53, f32[2048]{0:T(1024)S(1)} %get-tuple-element.58, f32[512]{0:T(512)S(1)} %get-tuple-element.54, ...), kind=kLoop, calls=%fused_computation.41 | loop fusion | flops 33554432 | bytes 16818192 | tf_op jit(solution)/shard_map/add | solution.py:127
  891.3 7.9 broadcast_in_dim.12
  899.2 22.7 %dynamic_update_slice.7 = f32[2,4096,512]{2,1,0:T(8,128)} dynamic-update-slice(f32[2,4096,512]{2,1,0:T(8,128)} %broadcast_in_dim.12, f32[2,2048,512]{2,1,0:T(8,128)} %pad_maximum_fusion, s32[]{:T(128)} %constant.100.clone.1, s32[]{:T(128)S(6)} %select_n.238, s32[]{:T(128)} %constant.100.clone.1) | dynamic-update-slice | bytes 16777220 | tf_op jit(solution)/shard_map/dynamic_update_slice | solution.py:130
  921.8 151.7 %reduce-scatter.2.cloned.1.call-done = f32[2,1024,512]{2,1,0:T(8,128)} async-done(((f32[2,4096,512]{2,1,0:T(8,128)}), f32[2,1024,512]{2,1,0:T(8,128)}) %reduce-scatter.2.cloned.1.call-update) | async-done | bytes 4194320 | tf_op jit(solution)/shard_map/reduce_scatter | solution.py:131
  1073.5 6.5 add.717
  (67 shorter events, 76.3 us)
Async XLA Ops:
  6.5 0.7 copy-start.6
  6.5 2.8 copy-start.5
  6.5 162.7 %all-gather.2.cloned.1.call-start = ((), (), s32[]{:S(2)}) async-start(), calls=%async_computation.3 | async-start | bytes 20971520 | tf_op jit(solution)/shard_map/all_gather | solution.py:85
  217.3 3.7 copy-start.3
  217.3 4.1 copy-start.4
  303.7 189.0 %all-to-all-start = ((f32[2,2048,512]{2,0,1:T(2,128)}), f32[2,2048,512]{2,0,1:T(2,128)}, u32[]{:S(2)}, u32[]{:S(2)}) async-start(f32[2,2048,512]{2,0,1:T(2,128)} %copy.148), calls=%async_computation | async-start | bytes 16777216 | tf_op jit(solution)/shard_map/all_to_all | solution.py:103
  519.5 9.7 copy-start.1
  540.8 3.1 copy-start.2
  545.6 9.1 copy-start
  582.1 188.8 %all-to-all-start.1 = ((f32[2,256,4096]{1,0,2:T(2,128)}), f32[2,256,4096]{1,0,2:T(2,128)}, u32[]{:S(2)}, u32[]{:S(2)}) async-start(f32[2,256,4096]{1,0,2:T(2,128)} %copy_dynamic-update-slice_fusion), calls=%async_computation.1 | async-start | bytes 16777216 | tf_op jit(solution)/shard_map/all_to_all | solution.py:123
  587.0 486.5 %reduce-scatter.2.cloned.1.call-start = ((), (), s32[]{:S(2)}) async-start(), calls=%async_computation.4 | async-start | bytes 20971520 | tf_op jit(solution)/shard_map/reduce_scatter | solution.py:131
Sparse Core Ops, SparseCore 0:
  9.2 160.0 all-gather.1
  922.0 151.5 reduce-scatter.1
where the time goes:
time: 1100 us; the launch traced here: 1090 us
  waiting for transfers between devices  630 us (57%)
  local copies, waits for them, and re-layouts  178 us (16%)
  matrix products  158 us (14%)
  other arithmetic  91.9 us (8%)
  between operations  19.3 us (2%)
    all_to_all x1, waiting for transfers between devices, on_device(): lax.all_to_all(padded, 'row', split_axis=2, concat_axis=1, tiled=True)  171 us
    all_to_all x1, waiting for transfers between devices, on_device(): lax.all_to_all(stacked, 'row', split_axis=1, concat_axis=2, tiled=True)  165 us
    reduce_scatter x1, waiting for transfers between devices, on_device(): summed = lax.psum_scatter(embedded, 'led', scatter_dimension=1, tiled=True)  152 us
    all_gather x1, waiting for transfers between devices, on_device(): region = lax.all_gather(spectrum, 'led', axis=1, tiled=True)  141 us
    dot_general x4, matrix products, transform(): jnp.einsum('p' + middle + ',pqkrj->q' + output, middle_pair, second_table...  79.1 us
    dot_general x4, matrix products, transform(): jnp.einsum('p' + inputs + ',pqtk->q' + middle, paired, first_table, preci...  78.8 us
    sub x1, other arithmetic, on_device(): lit_re = pupil_re * band_rows[0] - pupil_im * band_rows[1]  26.9 us
    another operation x4, local copies, waits for them, and re-layouts, on_device(): jnp.stack([lit_re, lit_im]).reshape(shape_rows)  24.9 us
  transfers between devices with their start and end apart: 4, of which 4 were waited for; matrix products, arithmetic and copies ran while one was open for 4% of the time, Pallas kernels for 0%

commit v1 on v0

--- a/solution.py
+++ b/solution.py
@@ -120,7 +120,12 @@
     padded = lax.dynamic_update_slice_in_dim(
         padded, back.reshape(2, block_rows, window), col_shift, 2
     )
-    gathered_cols = lax.all_to_all(padded, "row", split_axis=2, concat_axis=1, tiled=True)
+    gathered_cols = jnp.concatenate(
+        lax.all_to_all(
+            jnp.stack(jnp.split(padded, lax.axis_size("row"), axis=2), axis=0), "row", 0, 0
+        ),
+        axis=1,
+    )
     spec = transform(
         gathered_cols.reshape(shape_rows), "trc", "krc", "jkc", outer_rows, led_count, -1.0
     ).reshape(2, window, size_cols)

time: 1100 us -> 1190 us (1.082)
  local copies, waits for them, and re-layouts: 178 us -> 270 us
    dynamic_update_slice x1, local copies, waits for them, and re-layouts: 12.4 us -> 92.2 us  [on_device(): lax.dynamic_update_slice_in_dim(padded, back.reshape(2, block_rows, windo...]
    all_to_all x2 -> x0, local copies, waits for them, and re-layouts: 20.6 us -> none  [on_device(): lax.all_to_all(padded, 'row', split_axis=2, concat_axis=1, tiled=True)]
    unnamed x15 -> x22, local copies, waits for them, and re-layouts: 2.37 us -> 20.4 us
where the time goes in v1:
time: 1190 us; the launch traced here: 1180 us
  waiting for transfers between devices  630 us (53%)
  local copies, waits for them, and re-layouts  270 us (23%)
  matrix products  157 us (13%)
  other arithmetic  91.9 us (8%)
  between operations  19.3 us (2%)
    all_to_all x1, waiting for transfers between devices, on_device(): lax.all_to_all(jnp.stack(jnp.split(padded, lax.axis_size('row'), axis=2),...  171 us
    all_to_all x1, waiting for transfers between devices, on_device(): lax.all_to_all(stacked, 'row', split_axis=1, concat_axis=2, tiled=True)  165 us
    reduce_scatter x1, waiting for transfers between devices, on_device(): summed = lax.psum_scatter(embedded, 'led', scatter_dimension=1, tiled=True)  152 us
    all_gather x1, waiting for transfers between devices, on_device(): region = lax.all_gather(spectrum, 'led', axis=1, tiled=True)  141 us
    dynamic_update_slice x1, local copies, waits for them, and re-layouts, on_device(): lax.dynamic_update_slice_in_dim(padded, back.reshape(2, block_rows, windo...  92.2 us
    dot_general x4, matrix products, transform(): jnp.einsum('p' + middle + ',pqkrj->q' + output, middle_pair, second_table...  79.1 us
    dot_general x4, matrix products, transform(): jnp.einsum('p' + inputs + ',pqtk->q' + middle, paired, first_table, preci...  78.4 us
    sub x1, other arithmetic, on_device(): lit_re = pupil_re * band_rows[0] - pupil_im * band_rows[1]  26.9 us
  transfers between devices with their start and end apart: 4, of which 4 were waited for; matrix products, arithmetic and copies ran while one was open for 4% of the time, Pallas kernels for 0%

profile of v1, /device:TPU:0, one launch (start us, length us, event | category | flops | bytes accessed | tf_op | source)
XLA Modules:
  0.0 1178.1 jit_solution(17854127729474891173)
XLA Ops:
  27.8 141.4 %all-gather.2.cloned.1.call-done = f32[2,4096,512]{2,1,0:T(8,128)} async-done(((f32[2,1024,512]{2,1,0:T(8,128)}), f32[2,4096,512]{2,1,0:T(8,128)}) %all-gather.2.cloned.1.call-update) | async-done | bytes 16777232 | tf_op jit(solution)/shard_map/all_gather | solution.py:85
  169.3 26.9 %multiply_subtract_fusion = (f32[1,2048,512]{2,1,0:T(8,128)}, f32[1,2048,512]{2,1,0:T(8,128)}) fusion(f32[2,4096,512]{2,1,0:T(8,128)} %all-gather.2.cloned.1.call-done, s32[]{:T(128)S(6)} %select_n.238, s32[]{:T(128)S(6)} %add.718, f32[]{:T(128)} %bitcast.6, f32[512]{0:T(512)S(1)} %get-tuple-element.55, f32[2048]{0:T(1024)S(1)} %get-tuple-element.58, ...), kind=kLoop, calls=%fused_computation.54 | loop fusion | flops 33554432 | bytes 16818200 | tf_op jit(solution)/shard_map/sub | solution.py:90
  196.1 7.9 stack.242
  204.1 5.5 copy.86
  209.6 7.7 stack.243
  221.4 28.3 %fusion.46 = f32[2,512,4,512,1]{3,1,2,0,4:T(8,128)} fusion(f32[1,512,4,512]{3,1,0,2:T(8,128)S(1)} %copy.87, f32[1,512,4,512]{3,1,0,2:T(8,128)S(1)} %copy-done.3, f32[1,2,512,512]{2,3,0,1:T(8,128)S(1)} %copy-done.4, f32[1,2,512,512]{2,3,0,1:T(8,128)S(1)} %get-tuple-element.17), kind=kOutput, calls=%fused_computation.57 | convolution fusion | flops 25772949504 | bytes 20971520 | tf_op jit(solution)/shard_map/ptrc,pqtk->qkrc/dot_general | solution.py:55
  249.7 32.7 %fusion.11 = f32[2,4,512,512]{3,1,0,2:T(4,128)S(1)} fusion(f32[2,2,512,4,4]{3,4,0,1,2:T(4,128)} %copy.88, f32[2,512,4,512,1]{3,1,2,0,4:T(8,128)} %fusion.46), kind=kOutput, calls=%fused_computation.19 | convolution fusion | flops 201326592 | bytes 16908288 | tf_op jit(solution)/shard_map/pkrc,pqkrj->qjkc/dot_general | solution.py:58
  282.4 4.9 copy.90
  287.3 16.5 %copy.91 = f32[2,2048,512]{2,0,1:T(2,128)} copy(f32[2,2048,512]{2,1,0:T(8,128)S(1)} %bitcast.217) | data formatting | bytes 16777216 | tf_op jit(solution)/shard_map/reshape | solution.py:102
  303.7 5.1 all-to-all-start
  327.6 165.1 %all-to-all-done = f32[2,2048,512]{2,0,1:T(2,128)} async-done(((f32[2,2048,512]{2,0,1:T(2,128)}), f32[2,2048,512]{2,0,1:T(2,128)}, u32[]{:S(2)}, u32[]{:S(2)}) %all-to-all-start) | async-done | bytes 8388640 | tf_op jit(solution)/shard_map/all_to_all | solution.py:103
  492.7 8.2 copy.92
  501.0 8.8 copy.93
  509.8 4.5 dynamic-slice_bitcast_fusion
  514.3 5.3 copy.94
  519.5 9.7 fusion.54
  529.3 7.0 fusion.47
  545.6 9.1 fusion.53
  554.8 7.0 fusion.50
  561.8 4.4 copy.105
  566.2 7.4 copy.106
  573.6 7.5 broadcast_in_dim.15
  581.2 92.2 %dynamic_update_slice.6 = f32[2,256,4096]{2,0,1:T(2,128)} dynamic-update-slice(f32[2,256,4096]{2,0,1:T(2,128)} %broadcast_in_dim.15, f32[2,256,2048]{2,0,1:T(2,128)} %copy.106, s32[]{:T(128)} %constant.100.clone.1, s32[]{:T(128)} %constant.100.clone.1, s32[]{:T(128)S(6)} %select_n.239) | dynamic-update-slice | bytes 8388612 | tf_op jit(solution)/shard_map/dynamic_update_slice | solution.py:120
  694.0 5.0 all-to-all-start.1
  712.3 170.5 %all-to-all-done.1 = f32[8,2,256,512]{3,1,2,0:T(2,128)} async-done(((f32[8,2,256,512]{3,1,2,0:T(2,128)}), f32[8,2,256,512]{3,1,2,0:T(2,128)}, u32[]{:S(2)}, u32[]{:S(2)}) %all-to-all-start.1) | async-done | bytes 8388640 | tf_op jit(solution)/shard_map/all_to_all | solution.py:124
  882.8 31.2 %fusion.41 = f32[2,512,4,512,1]{3,1,2,0,4:T(8,128)} fusion(f32[2,512,4,512]{3,0,2,1:T(2,128)} %bitcast.75, f32[1,2,512,512]{2,3,1,0:T(8,128)} %get-tuple-element.16, f32[1,2,512,512]{2,3,1,0:T(8,128)S(1)} %get-tuple-element.15), kind=kOutput, calls=%fused_computation.56 | convolution fusion | flops 25770852352 | bytes 20971520 | tf_op jit(solution)/shard_map/ptrc,pqtk->qkrc/dot_general | solution.py:55
  914.1 32.4 %fusion.14 = f32[2,4,512,512]{3,1,0,2:T(4,128)S(1)} fusion(f32[2,2,512,4,4]{3,4,0,1,2:T(4,128)} %copy.109, f32[2,512,4,512,1]{3,1,2,0,4:T(8,128)} %fusion.41), kind=kOutput, calls=%fused_computation.20 | convolution fusion | flops 201326592 | bytes 16908288 | tf_op jit(solution)/shard_map/pkrc,pqkrj->qjkc/dot_general | solution.py:58
  954.8 23.1 %fusion.32 = (f32[1,2048,512]{2,1,0:T(8,128)S(1)}, f32[1,2048,512]{2,1,0:T(8,128)S(1)}) fusion(f32[1,4,512,512]{3,2,1,0:T(8,128)S(1)} %copy.112, f32[1,4,512,512]{3,2,1,0:T(8,128)S(1)} %copy.111, f32[]{:T(128)} %bitcast.6, f32[512]{0:T(512)S(1)} %get-tuple-element.55, f32[2048]{0:T(1024)S(1)} %get-tuple-element.58, f32[512]{0:T(512)S(1)} %get-tuple-element.56, ...), kind=kLoop, calls=%fused_computation.41 | loop fusion | flops 33554432 | bytes 16818192 | tf_op jit(solution)/shard_map/add | solution.py:132
  982.2 7.9 broadcast_in_dim.12
  990.1 22.7 %dynamic_update_slice.7 = f32[2,4096,512]{2,1,0:T(8,128)} dynamic-update-slice(f32[2,4096,512]{2,1,0:T(8,128)} %broadcast_in_dim.12, f32[2,2048,512]{2,1,0:T(8,128)} %pad_maximum_fusion, s32[]{:T(128)} %constant.100.clone.1, s32[]{:T(128)S(6)} %select_n.238, s32[]{:T(128)} %constant.100.clone.1) | dynamic-update-slice | bytes 16777220 | tf_op jit(solution)/shard_map/dynamic_update_slice | solution.py:135
  1012.7 151.8 %reduce-scatter.2.cloned.1.call-done = f32[2,1024,512]{2,1,0:T(8,128)} async-done(((f32[2,4096,512]{2,1,0:T(8,128)}), f32[2,1024,512]{2,1,0:T(8,128)}) %reduce-scatter.2.cloned.1.call-update) | async-done | bytes 4194320 | tf_op jit(solution)/shard_map/reduce_scatter | solution.py:136
  1164.5 6.5 add.717
  (74 shorter events, 94.5 us)
Async XLA Ops:
  6.5 0.7 copy-start.6
  6.5 2.8 copy-start.5
  6.5 162.7 %all-gather.2.cloned.1.call-start = ((), (), s32[]{:S(2)}) async-start(), calls=%async_computation.3 | async-start | bytes 20971520 | tf_op jit(solution)/shard_map/all_gather | solution.py:85
  217.3 3.7 copy-start.3
  217.3 4.1 copy-start.4
  303.7 189.0 %all-to-all-start = ((f32[2,2048,512]{2,0,1:T(2,128)}), f32[2,2048,512]{2,0,1:T(2,128)}, u32[]{:S(2)}, u32[]{:S(2)}) async-start(f32[2,2048,512]{2,0,1:T(2,128)} %copy.91), calls=%async_computation | async-start | bytes 16777216 | tf_op jit(solution)/shard_map/all_to_all | solution.py:103
  519.5 9.7 copy-start.1
  540.8 3.1 copy-start.2
  545.6 9.1 copy-start
  694.0 188.8 %all-to-all-start.1 = ((f32[8,2,256,512]{3,1,2,0:T(2,128)}), f32[8,2,256,512]{3,1,2,0:T(2,128)}, u32[]{:S(2)}, u32[]{:S(2)}) async-start(f32[8,2,256,512]{3,1,2,0:T(2,128)} %fusion.65), calls=%async_computation.1 | async-start | bytes 16777216 | tf_op jit(solution)/shard_map/all_to_all | solution.py:124
  699.0 465.5 %reduce-scatter.2.cloned.1.call-start = ((), (), s32[]{:S(2)}) async-start(), calls=%async_computation.4 | async-start | bytes 20971520 | tf_op jit(solution)/shard_map/reduce_scatter | solution.py:136
Sparse Core Ops, SparseCore 0:
  9.2 160.0 all-gather.1
  1012.9 151.6 reduce-scatter.1
